TPU v7x, 32 devices: a whole 2x2x4 slice. The times are simulated.
32 devices in a mesh: cand: 4 (over y, x), hist: 8 (over z, core).
Axes of the slice: x: 2, y: 2, z: 4, core: 2. Of those that a mesh axis runs over, the one named last changes fastest.
Arguments:
- cand_x: bfloat16 [2, 1024, 1024], P(None, ('cand', 'hist')), may hold values from -6 to 6
- qu_weight: bfloat16 [1024, 2048], replicated, may hold values from -0.1875 to 0.1875
- out_weight: bfloat16 [1024, 1024], replicated, may hold values from -0.1875 to 0.1875
- k_cache: bfloat16 [131072, 1024], P('hist', 'cand'), may hold values from -1.5 to 1.5
- v_cache: bfloat16 [131072, 1024], P('hist', 'cand'), may hold values from -6 to 6
- hist_len: int32 [16], replicated, may hold values from 1 to 32768, as said below
- cand_count: int32 [2, 16], replicated, may hold values from 1 to 128, 1024 in all within a row
- tile_user: int32 [1024], P('hist'), may hold values from 0 to 16, as said below
- tile_rank: int32 [1024], P('hist'), may hold values from 0 to 255, as said below
Outputs:
- ranked: bfloat16 [2, 1024, 1024], P(None, ('cand', 'hist'))
Inputs may be any that keep to these rules, and one draw needn't show every extreme that they name: A user's history fills exactly ceil(hist_len / 128) tile slots; one user's history is 32768 rows long. `tile_user`: slot owner, 16 for an empty slot; within each hist index's 128 slots the occupied ones come first; every user owns at least one slot. `tile_rank`: each tile position 0 to ceil(hist_len[u] / 128) - 1 of every user u stands in exactly one slot; empty slots hold 0. `cand_count`: row m gives the candidates of each user in micro-batch m, numbered user by user; they sum to 1024 and one user has exactly 128.
All inputs are finite; a program needn't handle non-finite values.
Results may differ from a plain program's by a relative error of at most 0.0051.
Values may be sent and summed in bfloat16 or wider, within the bound.
No kernel may reach another device: no remote copies, remote signals or barrier semaphores. Data moves between devices by JAX's collectives and lax.ppermute only.
A program may use at most 128 MiB of HBM per device.

v0:
```python
import jax
import jax.numpy as jnp
from jax import lax
from jax.sharding import PartitionSpec as P

HEAD_DIM = 128
TILE = 128
USERS = 16
MICRO = 2
EPSILON = 1e-06


def body(
    cand_x, qu_weight, out_weight, k_cache, v_cache, hist_len, cand_count, tile_user, tile_rank
):
    n_cand = lax.axis_size("cand")
    n_hist = lax.axis_size("hist")
    local_rows = cand_x.shape[1]
    model_width = cand_x.shape[2]
    head_cols = k_cache.shape[1]
    heads_here = head_cols // HEAD_DIM
    key_tiles = k_cache.reshape(-1, TILE, heads_here, HEAD_DIM)
    value_tiles = v_cache.reshape(-1, TILE, heads_here, HEAD_DIM)
    tiles_here = key_tiles.shape[0]
    per_turn = max(tiles_here // 8, 1)
    turn_count = tiles_here // per_turn
    user_ids = jnp.arange(USERS, dtype=jnp.int32)
    tile_rows = jnp.arange(TILE, dtype=jnp.int32)
    outputs = []
    for micro_index in range(MICRO):
        cand_rows = cand_x[micro_index]
        projected = jax.nn.silu(jnp.dot(cand_rows, qu_weight, preferred_element_type=jnp.float32))
        queries = projected[:, :model_width].astype(jnp.bfloat16)
        gate_vals = projected[:, model_width:].astype(jnp.bfloat16)
        gathered = lax.all_gather(queries, "hist", axis=0, tiled=True)
        queries_all = lax.all_to_all(gathered, "cand", split_axis=1, concat_axis=0, tiled=True)
        all_cands = queries_all.shape[0]
        window = 2 * all_cands // USERS
        counts = cand_count[micro_index]
        cand_start = jnp.cumsum(counts) - counts
        user_offsets = jnp.minimum(cand_start, all_cands - window)
        user_windows = jnp.stack(
            [
                lax.dynamic_slice_in_dim(queries_all, user_offsets[member], window, 0)
                for member in range(USERS)
            ]
        )
        row_ids = jnp.arange(window, dtype=jnp.int32)

        def visit_tiles(turn_index, user_sums):
            first_slot = turn_index * per_turn
            key_block = lax.dynamic_slice_in_dim(key_tiles, first_slot, per_turn, 0)
            value_block = lax.dynamic_slice_in_dim(value_tiles, first_slot, per_turn, 0)
            owners = lax.dynamic_slice_in_dim(tile_user, first_slot, per_turn, 0)
            positions = lax.dynamic_slice_in_dim(tile_rank, first_slot, per_turn, 0)
            matches = owners[:, None] == user_ids[None, :]
            length = jnp.sum(jnp.where(matches, hist_len[None, :], 0), axis=1)
            first_cand = jnp.sum(jnp.where(matches, cand_start[None, :], 0), axis=1)
            cand_total = jnp.sum(jnp.where(matches, counts[None, :], 0), axis=1)
            offsets = jnp.sum(jnp.where(matches, user_offsets[None, :], 0), axis=1)
            windows = jnp.einsum(
                "gu,uwc->gwc",
                matches.astype(jnp.bfloat16),
                user_windows,
                preferred_element_type=jnp.float32,
            ).astype(jnp.bfloat16)
            windows = windows.reshape(per_turn, window, heads_here, HEAD_DIM)
            scores = jnp.einsum(
                "gwhd,gkhd->ghwk", windows, key_block, preferred_element_type=jnp.float32
            )
            cand_ids = offsets[:, None] + row_ids[None, :]
            cand_ok = (cand_ids >= first_cand[:, None]) & (
                cand_ids < (first_cand + cand_total)[:, None]
            )
            key_ok = positions[:, None] * TILE + tile_rows[None, :] < length[:, None]
            keep_mask = cand_ok[:, None, :, None] & key_ok[:, None, None, :]
            weights = jnp.where(keep_mask, jax.nn.silu(scores), 0.0).astype(jnp.bfloat16)
            contrib = jnp.einsum(
                "ghwk,gkhd->gwhd", weights, value_block, preferred_element_type=jnp.float32
            )
            contrib = contrib.reshape(per_turn, window, head_cols)
            added = jnp.einsum(
                "gu,gwc->uwc", matches.astype(jnp.float32), contrib, precision=lax.Precision.HIGHEST
            )
            return user_sums + added

        user_sums = lax.fori_loop(
            0, turn_count, visit_tiles, jnp.zeros((USERS, window, head_cols), jnp.float32)
        )
        partial_value = jnp.zeros((all_cands, head_cols), jnp.float32)
        for member in range(USERS):
            current = lax.dynamic_slice_in_dim(partial_value, user_offsets[member], window, 0)
            partial_value = lax.dynamic_update_slice_in_dim(
                partial_value, current + user_sums[member], user_offsets[member], 0
            )
        blocks = partial_value.reshape(n_cand, n_hist, local_rows, head_cols)
        regrouped = lax.all_to_all(blocks, "cand", split_axis=0, concat_axis=3, tiled=True)
        attended = lax.psum_scatter(regrouped, "hist", scatter_dimension=1, tiled=True)
        attended = attended.reshape(local_rows, model_width)
        average = jnp.mean(attended, axis=-1, keepdims=True)
        centered = attended - average
        spread_sq = jnp.mean(centered * centered, axis=-1, keepdims=True)
        normed = centered * lax.rsqrt(spread_sq + EPSILON)
        mixed_rows = (normed * gate_vals.astype(jnp.float32)).astype(jnp.bfloat16)
        ranked = jnp.dot(
            mixed_rows, out_weight, preferred_element_type=jnp.float32
        ) + cand_rows.astype(jnp.float32)
        outputs.append(ranked.astype(jnp.bfloat16))
    return jnp.stack(outputs)


def solution(mesh):
    return jax.shard_map(
        body,
        mesh=mesh,
        in_specs=(
            P(None, ("cand", "hist"), None),
            P(),
            P(),
            P("hist", "cand"),
            P("hist", "cand"),
            P(),
            P(),
            P("hist"),
            P("hist"),
        ),
        out_specs=P(None, ("cand", "hist"), None),
        check_vma=False,
    )
```

profile of v0, /device:TPU:0, one launch (start us, length us, event | category | flops | bytes accessed | tf_op | source)
XLA Modules:
  0.0 606.1 jit_solution(5571507034580627950)
XLA Ops:
  9.8 16.7 %all_gather.6 = bf16[256,1024]{1,0:T(8,128)(2,1)S(1)} all-gather(bf16[32,1024]{1,0:T(8,128)(2,1)S(1)} %slice.354), channel_id=1, replica_groups=mesh['cand'=4,'hist'=8] {'hist'}, dimensions={0}, use_global_device_ids=true | all-gather | bytes 589824 | tf_op jit(solution)/shard_map/all_gather | solution.py:35
  76.7 12.5 %reshape.390 = bf16[128,128,2,128]{3,2,1,0:T(2,128)(2,1)} reshape(bf16[16384,256]{1,0:T(8,128)(2,1)} %param.17) | data formatting | bytes 16777216 | tf_op jit(solution)/shard_map/reshape | solution.py:23
  89.3 20.7 %copy.112 = bf16[128,128,2,128]{1,3,2,0:T(8,128)(2,1)} copy(bf16[128,128,2,128]{3,2,1,0:T(2,128)(2,1)} %reshape.390) | data formatting | bytes 16777216
  110.0 12.5 %reshape.391 = bf16[128,128,2,128]{3,2,1,0:T(2,128)(2,1)} reshape(bf16[16384,256]{1,0:T(8,128)(2,1)} %param.16) | data formatting | bytes 16777216 | tf_op jit(solution)/shard_map/reshape | solution.py:22
  122.5 9.1 %copy.114 = bf16[128,128,2,128]{3,1,2,0:T(8,128)(2,1)} copy(bf16[128,128,2,128]{3,2,1,0:T(2,128)(2,1)} %reshape.391) | data formatting | bytes 16777216
  131.7 14.8 %all_gather.7 = bf16[256,1024]{1,0:T(8,128)(2,1)S(1)} all-gather(bf16[32,1024]{1,0:T(8,128)(2,1)S(1)} %slice.372), channel_id=1, replica_groups=mesh['cand'=4,'hist'=8] {'hist'}, dimensions={0}, use_global_device_ids=true | all-gather | bytes 589824 | tf_op jit(solution)/shard_map/all_gather | solution.py:35
  173.6 129.4 %while.32 = (s32[]{:T(128)}, f32[16,128,256]{2,0,1:T(8,128)}, s32[128]{0:T(128)S(1)}, bf16[128,128,2,128]{1,3,2,0:T(8,128)(2,1)}, s32[16]{0:T(128)S(1)}, /*index...) while((s32[]{:T(128)}, f32[16,128,256]{2,0,1:T(8,128)}, ...), condition=%wide.region_6.7_spmd.clone.clone, body=%wide.region_1.6_spmd.clone.clone.sunk | while | flops 390871776 | bytes 20463428 | solution.py:87
  177.1 4.8 fusion.165
  192.8 4.8 fusion.165
  209.0 4.8 fusion.165
  225.3 4.8 fusion.165
  241.6 4.8 fusion.165
  257.8 4.8 fusion.165
  274.1 4.8 fusion.165
  290.3 4.8 fusion.165
  370.7 130.0 %while.33 = (s32[]{:T(128)}, f32[16,128,256]{2,0,1:T(8,128)}, s32[128]{0:T(128)S(1)}, bf16[128,128,2,128]{1,3,2,0:T(8,128)(2,1)}, s32[16]{0:T(128)S(1)}, /*index...) while((s32[]{:T(128)}, f32[16,128,256]{2,0,1:T(8,128)}, ...), condition=%wide.region_16.17_spmd.clone.clone, body=%wide.region_11.16_spmd.clone.clone.sunk | while | flops 390871776 | bytes 20467012 | solution.py:87
  374.2 4.8 fusion.175
  397.9 4.8 select_add_fusion.5
  406.3 4.8 fusion.175
  414.2 4.8 select_add_fusion.5
  422.6 4.8 fusion.175
  430.5 4.8 select_add_fusion.5
  438.9 4.8 fusion.175
  446.9 4.8 select_add_fusion.5
  455.3 4.8 fusion.175
  463.2 4.8 select_add_fusion.5
  471.6 4.8 fusion.175
  479.5 4.8 select_add_fusion.5
  488.0 4.8 fusion.175
  495.9 4.8 select_add_fusion.5
  537.2 18.7 %all_to_all.74 = f32[4,8,32,256]{3,2,1,0:T(8,128)S(1)} all-to-all(f32[4,8,32,256]{3,2,1,0:T(8,128)S(1)} %bitcast.340), channel_id=1, replica_groups=mesh['cand'=4,'hist'=8] {'cand'}, dimensions={0} | all-to-all | bytes 2097152 | tf_op jit(solution)/shard_map/all_to_all | solution.py:97
  563.5 30.9 %reduce-scatter.5.cloned.1.call-done = f32[1,1,32,1024]{3,2,1,0:T(8,128)} async-done(((f32[1,8,32,1024]{3,2,1,0:T(8,128)}), f32[1,1,32,1024]{3,2,1,0:T(8,128)}) %reduce-scatter.5.cloned.1.call-update) | async-done | bytes 131088 | tf_op jit(solution)/shard_map/reduce_scatter | solution.py:98
  (521 shorter events, 290.2 us)
Async XLA Ops:
  6.5 590.1 %copy-start = (bf16[1024,1024]{1,0:T(8,128)(2,1)S(1)}, bf16[1024,1024]{1,0:T(8,128)(2,1)}, u32[]{:S(2)}) copy-start(bf16[1024,1024]{1,0:T(8,128)(2,1)} %param.15) | copy-start | bytes 6291460
  9.8 17.6 %copy-start.5 = (bf16[32,2048]{1,0:T(8,128)(2,1)}, bf16[32,2048]{1,0:T(8,128)(2,1)S(1)}, u32[]{:S(2)}) copy-start(bf16[32,2048]{1,0:T(8,128)(2,1)S(1)} %multiply_convert_fusion.1) | copy-start | bytes 393220
  9.8 21.3 %copy-start.4 = (bf16[2,32,1024]{2,1,0:T(8,128)(2,1)S(1)}, bf16[2,32,1024]{2,1,0:T(8,128)(2,1)}, u32[]{:S(2)}) copy-start(bf16[2,32,1024]{2,1,0:T(8,128)(2,1)} %param.13) | copy-start | bytes 393220
  27.4 139.7 %all-to-all-start = ((bf16[256,4,256]{2,0,1:T(8,128)(2,1)}), bf16[256,4,256]{2,0,1:T(8,128)(2,1)S(1)}, u32[]{:S(2)}, u32[]{:S(2)}) async-start(bf16[256,4,256]{2,0,1:T(8,128)(2,1)} %bitcast.313), calls=%async_computation | async-start | bytes 1048576 | tf_op jit(solution)/shard_map/all_to_all | solution.py:36
  34.2 97.5 %copy-start.7 = (bf16[32,2048]{1,0:T(8,128)(2,1)}, bf16[32,2048]{1,0:T(8,128)(2,1)S(1)}, u32[]{:S(2)}) copy-start(bf16[32,2048]{1,0:T(8,128)(2,1)S(1)} %multiply_convert_fusion) | copy-start | bytes 393220
  167.0 182.9 %all-to-all-start.2 = ((bf16[256,4,256]{2,0,1:T(8,128)(2,1)}), bf16[256,4,256]{2,0,1:T(8,128)(2,1)}, u32[]{:S(2)}, u32[]{:S(2)}) async-start(bf16[256,4,256]{2,0,1:T(8,128)(2,1)} %bitcast.312), calls=%async_computation.3 | async-start | bytes 1048576 | tf_op jit(solution)/shard_map/all_to_all | solution.py:36
  349.9 174.8 %all-to-all-start.1 = ((f32[4,8,32,256]{3,2,1,0:T(8,128)}), f32[4,8,32,256]{3,2,1,0:T(8,128)}, u32[]{:S(2)}, u32[]{:S(2)}) async-start(f32[4,8,32,256]{3,2,1,0:T(8,128)} %bitcast.54), calls=%async_computation.1 | async-start | bytes 2097152 | tf_op jit(solution)/shard_map/all_to_all | solution.py:97
  354.2 207.2 %reduce-scatter.3.cloned.1.call-start = ((), (), s32[]{:S(2)}) async-start(), calls=%async_computation.6 | async-start | bytes 1179648 | tf_op jit(solution)/shard_map/reduce_scatter | solution.py:98
  354.5 16.2 %copy-start.10 = (s32[1,16]{1,0:T(1,128)S(1)}, s32[1,16]{1,0:T(1,128)}, u32[]{:S(2)}) copy-start(s32[1,16]{1,0:T(1,128)} %get-tuple-element.955) | copy-start | bytes 196
  354.5 16.2 %copy-start.14 = (s32[16]{0:T(128)S(1)}, s32[16]{0:T(128)}, u32[]{:S(2)}) copy-start(s32[16]{0:T(128)} %get-tuple-element.954) | copy-start | bytes 196
  397.9 4.8 copy-start.22
  397.9 4.8 copy-start.26
  414.2 4.8 copy-start.22
  414.2 4.8 copy-start.26
  430.5 4.8 copy-start.15
  430.5 4.8 copy-start.22
  430.5 4.8 copy-start.26
  446.9 4.8 copy-start.15
  446.9 4.8 copy-start.22
  446.9 4.8 copy-start.26
  463.2 4.8 copy-start.15
  463.2 4.8 copy-start.22
  463.2 4.8 copy-start.26
  479.5 4.8 copy-start.15
  479.5 4.8 copy-start.22
  479.5 4.8 copy-start.26
  495.9 4.8 copy-start.15
  495.9 4.8 copy-start.22
  495.9 4.8 copy-start.26
  527.1 67.3 %reduce-scatter.5.cloned.1.call-start = ((), (), s32[]{:S(2)}) async-start(), calls=%async_computation.7 | async-start | bytes 1179648 | tf_op jit(solution)/shard_map/reduce_scatter | solution.py:98
  555.8 40.8 %copy-start.6 = (bf16[32,2048]{1,0:T(8,128)(2,1)S(1)}, bf16[32,2048]{1,0:T(8,128)(2,1)}, u32[]{:S(2)}) copy-start(bf16[32,2048]{1,0:T(8,128)(2,1)} %copy-done.5) | copy-start | bytes 393220
  557.0 41.1 %copy-start.8 = (bf16[32,2048]{1,0:T(8,128)(2,1)S(1)}, bf16[32,2048]{1,0:T(8,128)(2,1)}, u32[]{:S(2)}) copy-start(bf16[32,2048]{1,0:T(8,128)(2,1)} %copy-done.7) | copy-start | bytes 393220
  (84 other events, 247.2 us)
Sparse Core Ops, SparseCore 0:
  527.3 34.0 reduce-scatter.2
  563.7 30.6 reduce-scatter.4
where the time goes:
time: 612 us; the launch traced here: 606 us
  local copies, waits for them, and re-layouts  203 us (33%)
  matrix products  186 us (30%)
  between operations  73.4 us (12%)
  blocking collectives  50.2 us (8%)
  other arithmetic  43.3 us (7%)
  waiting for transfers between devices  35.3 us (6%)
  starting transfers between devices  12.6 us (2%)
    dot_general x16, matrix products, visit_tiles(): jnp.einsum('ghwk,gkhd->gwhd', weights, value_block, preferred_element_typ...  76.4 us
    dot_general x16, matrix products, visit_tiles(): jnp.einsum('gu,gwc->uwc', matches.astype(jnp.float32), contrib, precision...  74.5 us
    reshape x16, local copies, waits for them, and re-layouts, visit_tiles(): contrib = contrib.reshape(per_turn, window, head_cols)  50.3 us
    unnamed x64, local copies, waits for them, and re-layouts  49.8 us
    dynamic_update_slice x32, local copies, waits for them, and re-layouts, body(): lax.dynamic_update_slice_in_dim(partial_value, current + user_sums[member...  42 us
    reduce_scatter x2, waiting for transfers between devices, body(): lax.psum_scatter(regrouped, 'hist', scatter_dimension=1, tiled=True)  35.2 us
    all_gather x2, blocking collectives, body(): gathered = lax.all_gather(queries, 'hist', axis=0, tiled=True)  31.5 us
    add x30, other arithmetic, body(): current + user_sums[member]  27.9 us
  transfers between devices with their start and end apart: 5, of which 2 were waited for; matrix products, arithmetic and copies ran while one was open for 69% of the time, Pallas kernels for 0%

commit v1 on v0

--- a/solution.py
+++ b/solution.py
@@ -8,6 +8,24 @@
 USERS = 16
 MICRO = 2
 EPSILON = 1e-06
+
+
+def collect(shard, axis, dim):
+    ways, here, hop = (lax.axis_size(axis), lax.axis_index(axis), shard.shape[dim])
+    shape = [n * ways if d == dim else n for d, n in enumerate(shard.shape)]
+    full = lax.dynamic_update_slice_in_dim(
+        jnp.zeros(shape, shard.dtype), shard, here * hop, axis=dim
+    )
+    going_up = going_down = shard
+    for far in range(1, ways // 2 + 1):
+        going_up = lax.ppermute(going_up, axis, [(d, (d + 1) % ways) for d in range(ways)])
+        full = lax.dynamic_update_slice_in_dim(full, going_up, (here - far) % ways * hop, axis=dim)
+        if 2 * far < ways:
+            going_down = lax.ppermute(going_down, axis, [(d, (d - 1) % ways) for d in range(ways)])
+            full = lax.dynamic_update_slice_in_dim(
+                full, going_down, (here + far) % ways * hop, axis=dim
+            )
+    return full
 
 
 def body(
@@ -32,7 +50,7 @@
         projected = jax.nn.silu(jnp.dot(cand_rows, qu_weight, preferred_element_type=jnp.float32))
         queries = projected[:, :model_width].astype(jnp.bfloat16)
         gate_vals = projected[:, model_width:].astype(jnp.bfloat16)
-        gathered = lax.all_gather(queries, "hist", axis=0, tiled=True)
+        gathered = collect(queries, "hist", 0)
         queries_all = lax.all_to_all(gathered, "cand", split_axis=1, concat_axis=0, tiled=True)
         all_cands = queries_all.shape[0]
         window = 2 * all_cands // USERS

time: 612 us -> 652 us (1.065)
  local copies, waits for them, and re-layouts: 203 us -> 252 us
  blocking collectives: 50.2 us -> 15 us
  starting transfers between devices: 12.6 us -> 33.3 us
  waiting for transfers between devices: 35.3 us -> 42.5 us
    dynamic_update_slice x0 -> x16, local copies, waits for them, and re-layouts: none -> 54.9 us  [the longest x8 25.1 us: collect(): lax.dynamic_update_slice_in_dim(full, going_up, (here - far) % ways * hop...]
    all_gather x2 -> x0, blocking collectives: 31.5 us -> none  [body(): gathered = lax.all_gather(queries, 'hist', axis=0, tiled=True)]
    ppermute x0 -> x14, starting transfers between devices: none -> 19.7 us  [the longest x6 18.6 us: collect(): lax.ppermute(going_down, axis, [(d, (d - 1) % ways) for d in range(ways)])]
    unnamed x64 -> x66, local copies, waits for them, and re-layouts: 49.8 us -> 37.2 us
  transfers between devices with their start and end apart: 5 -> 19, of which waited for: 2 -> 4; matrix products, arithmetic and copies ran while one was open for 69% -> 72% of each run, Pallas kernels for 0% -> 0%
where the time goes in v1:
time: 652 us; the launch traced here: 647 us
  local copies, waits for them, and re-layouts  252 us (39%)
  matrix products  185 us (28%)
  between operations  74.3 us (11%)
  other arithmetic  43.4 us (7%)
  waiting for transfers between devices  42.5 us (7%)
  starting transfers between devices  33.3 us (5%)
  blocking collectives  15 us (2%)
    dot_general x16, matrix products, visit_tiles(): jnp.einsum('ghwk,gkhd->gwhd', weights, value_block, preferred_element_typ...  76.8 us
    dot_general x16, matrix products, visit_tiles(): jnp.einsum('gu,gwc->uwc', matches.astype(jnp.float32), contrib, precision...  74.6 us
    reshape x16, local copies, waits for them, and re-layouts, visit_tiles(): contrib = contrib.reshape(per_turn, window, head_cols)  50.3 us
    dynamic_update_slice x32, local copies, waits for them, and re-layouts, body(): lax.dynamic_update_slice_in_dim(partial_value, current + user_sums[member...  42.1 us
    reduce_scatter x2, waiting for transfers between devices, body(): lax.psum_scatter(regrouped, 'hist', scatter_dimension=1, tiled=True)  38.5 us
    unnamed x66, local copies, waits for them, and re-layouts  37.2 us
    add x30, other arithmetic, body(): current + user_sums[member]  27.9 us
    dot_general x16, matrix products, visit_tiles(): jnp.einsum('gu,uwc->gwc', matches.astype(jnp.bfloat16), user_windows, pre...  27.2 us
  transfers between devices with their start and end apart: 19, of which 4 were waited for; matrix products, arithmetic and copies ran while one was open for 72% of the time, Pallas kernels for 0%

profile of v1, /device:TPU:0, one launch (start us, length us, event | category | flops | bytes accessed | tf_op | source)
XLA Modules:
  0.0 646.5 jit_solution(7767348813571627145)
XLA Ops:
  112.6 12.5 %reshape.390 = bf16[128,128,2,128]{3,2,1,0:T(2,128)(2,1)} reshape(bf16[16384,256]{1,0:T(8,128)(2,1)} %param.17) | data formatting | bytes 16777216 | tf_op jit(solution)/shard_map/reshape | solution.py:41
  125.1 20.7 %copy.201 = bf16[128,128,2,128]{1,3,2,0:T(8,128)(2,1)} copy(bf16[128,128,2,128]{3,2,1,0:T(2,128)(2,1)} %reshape.390) | data formatting | bytes 16777216
  145.9 12.6 %reshape.391 = bf16[128,128,2,128]{3,2,1,0:T(2,128)(2,1)} reshape(bf16[16384,256]{1,0:T(8,128)(2,1)} %param.16) | data formatting | bytes 16777216 | tf_op jit(solution)/shard_map/reshape | solution.py:40
  158.5 9.2 %copy.203 = bf16[128,128,2,128]{3,1,2,0:T(8,128)(2,1)} copy(bf16[128,128,2,128]{3,2,1,0:T(2,128)(2,1)} %reshape.391) | data formatting | bytes 16777216
  223.9 131.1 %while.32 = (s32[]{:T(128)}, f32[16,128,256]{2,0,1:T(8,128)}, s32[128]{0:T(128)S(1)}, bf16[128,128,2,128]{1,3,2,0:T(8,128)(2,1)}, s32[16]{0:T(128)S(1)}, /*index...) while((s32[]{:T(128)}, f32[16,128,256]{2,0,1:T(8,128)}, ...), condition=%wide.region_6.7_spmd.clone.clone, body=%wide.region_1.6_spmd.clone.clone.sunk | while | flops 390871776 | bytes 20463428 | solution.py:105
  227.7 4.8 fusion.165
  243.5 4.8 fusion.165
  260.0 4.8 fusion.165
  276.4 4.8 fusion.165
  292.9 4.8 fusion.165
  309.4 4.8 fusion.165
  325.8 4.8 fusion.165
  342.3 4.8 fusion.165
  410.0 131.5 %while.33 = (s32[]{:T(128)}, f32[16,128,256]{2,0,1:T(8,128)}, s32[128]{0:T(128)S(1)}, bf16[128,128,2,128]{1,3,2,0:T(8,128)(2,1)}, s32[16]{0:T(128)S(1)}, /*index...) while((s32[]{:T(128)}, f32[16,128,256]{2,0,1:T(8,128)}, ...), condition=%wide.region_16.17_spmd.clone.clone, body=%wide.region_11.16_spmd.clone.clone.sunk | while | flops 390871776 | bytes 20467012 | solution.py:105
  413.8 4.8 fusion.175
  429.6 4.8 fusion.175
  437.6 4.7 select_add_fusion.5
  446.2 4.8 fusion.175
  454.1 4.7 select_add_fusion.5
  462.7 4.8 fusion.175
  470.6 4.7 select_add_fusion.5
  479.2 4.8 fusion.175
  487.2 4.7 select_add_fusion.5
  495.7 4.8 fusion.175
  503.7 4.7 select_add_fusion.5
  512.2 4.8 fusion.175
  520.2 4.7 select_add_fusion.5
  528.8 4.8 fusion.175
  536.7 4.7 select_add_fusion.5
  578.0 15.0 %all_to_all.74 = f32[4,8,32,256]{3,2,1,0:T(8,128)S(1)} all-to-all(f32[4,8,32,256]{3,2,1,0:T(8,128)S(1)} %bitcast.332), channel_id=1, replica_groups=mesh['cand'=4,'hist'=8] {'cand'}, dimensions={0} | all-to-all | bytes 2097152 | tf_op jit(solution)/shard_map/all_to_all | solution.py:115
  594.2 7.8 %reduce-scatter.3.cloned.1.call-done = f32[1,1,32,1024]{3,2,1,0:T(8,128)} async-done(((f32[1,8,32,1024]{3,2,1,0:T(8,128)}), f32[1,1,32,1024]{3,2,1,0:T(8,128)}) %reduce-scatter.3.cloned.1.call-update) | async-done | bytes 131088 | tf_op jit(solution)/shard_map/reduce_scatter | solution.py:116
  604.1 30.7 %reduce-scatter.5.cloned.1.call-done = f32[1,1,32,1024]{3,2,1,0:T(8,128)} async-done(((f32[1,8,32,1024]{3,2,1,0:T(8,128)}), f32[1,1,32,1024]{3,2,1,0:T(8,128)}) %reduce-scatter.5.cloned.1.call-update) | async-done | bytes 131088 | tf_op jit(solution)/shard_map/reduce_scatter | solution.py:116
  (583 shorter events, 352.3 us)
Async XLA Ops:
  6.5 630.5 %copy-start = (bf16[1024,1024]{1,0:T(8,128)(2,1)S(1)}, bf16[1024,1024]{1,0:T(8,128)(2,1)}, u32[]{:S(2)}) copy-start(bf16[1024,1024]{1,0:T(8,128)(2,1)} %param.15) | copy-start | bytes 6291460
  6.5 15.4 %copy-start.5 = (bf16[2,32,1024]{2,1,0:T(8,128)(2,1)S(1)}, bf16[2,32,1024]{2,1,0:T(8,128)(2,1)}, u32[]{:S(2)}) copy-start(bf16[2,32,1024]{2,1,0:T(8,128)(2,1)} %param.13) | copy-start | bytes 393220
  6.5 15.4 %copy-start.1 = (bf16[1024,2048]{1,0:T(8,128)(2,1)S(1)}, bf16[1024,2048]{1,0:T(8,128)(2,1)}, u32[]{:S(2)}) copy-start(bf16[1024,2048]{1,0:T(8,128)(2,1)} %param.14) | copy-start | bytes 12582916
  9.8 13.0 %copy-start.6 = (bf16[32,2048]{1,0:T(8,128)(2,1)}, bf16[32,2048]{1,0:T(8,128)(2,1)S(1)}, u32[]{:S(2)}) copy-start(bf16[32,2048]{1,0:T(8,128)(2,1)S(1)} %multiply_convert_fusion.1) | copy-start | bytes 393220
  9.8 17.7 %copy-start.19 = (s32[2,16]{1,0:T(2,128)S(1)}, s32[2,16]{1,0:T(2,128)}, u32[]{:S(2)}) copy-start(s32[2,16]{1,0:T(2,128)} %param.19) | copy-start | bytes 388
  9.8 6.5 %collective-permute-start = (bf16[32,1024]{1,0:T(8,128)(2,1)S(1)}, bf16[32,1024]{1,0:T(8,128)(2,1)S(1)}, u32[]{:S(2)}, u32[]{:S(2)}) collective-permute-start(bf16[32,1024]{1,0:T(8,128)(2,1)S(1)} %slice.354), channel_id=1, source_target_pairs={{0,1},{1,2},{2,3},{3,4},{4,5},{5,6},{6,7},{7,0},{8,9},{9,10},{10,1... | collective-permute-start | bytes 196616 | tf_op jit(solution)/shard_map/ppermute | solution.py:21
  10.3 6.0 collective-permute-start.1
  16.3 5.6 collective-permute-start.2
  16.3 10.7 %collective-permute-start.3 = (bf16[32,1024]{1,0:T(8,128)(2,1)S(1)}, bf16[32,1024]{1,0:T(8,128)(2,1)S(1)}, u32[]{:S(2)}, u32[]{:S(2)}) collective-permute-start(bf16[32,1024]{1,0:T(8,128)(2,1)S(1)} %collective-permute-done.1), channel_id=1, source_target_pairs={{0,7},{1,0},{2,1},{3,2},{4,3},{5,4},{6,5},{7,6},{8,15},{9,8},{10,9... | collective-permute-start | bytes 196616 | tf_op jit(solution)/shard_map/ppermute | solution.py:24
  21.9 5.6 collective-permute-start.4
  23.4 17.1 %collective-permute-start.7 = (bf16[32,1024]{1,0:T(8,128)(2,1)S(1)}, bf16[32,1024]{1,0:T(8,128)(2,1)S(1)}, u32[]{:S(2)}, u32[]{:S(2)}) collective-permute-start(bf16[32,1024]{1,0:T(8,128)(2,1)S(1)} %slice.372), channel_id=1, source_target_pairs={{0,1},{1,2},{2,3},{3,4},{4,5},{5,6},{6,7},{7,0},{8,9},{9,10},{10,1... | collective-permute-start | bytes 196616 | tf_op jit(solution)/shard_map/ppermute | solution.py:21
  23.4 40.7 %collective-permute-start.8 = (bf16[32,1024]{1,0:T(8,128)(2,1)S(1)}, bf16[32,1024]{1,0:T(8,128)(2,1)S(1)}, u32[]{:S(2)}, u32[]{:S(2)}) collective-permute-start(bf16[32,1024]{1,0:T(8,128)(2,1)S(1)} %slice.372), channel_id=1, source_target_pairs={{0,7},{1,0},{2,1},{3,2},{4,3},{5,4},{6,5},{7,6},{8,15},{9,8},{10,9... | collective-permute-start | bytes 196616 | tf_op jit(solution)/shard_map/ppermute | solution.py:24
  27.0 25.0 %collective-permute-start.5 = (bf16[32,1024]{1,0:T(8,128)(2,1)S(1)}, bf16[32,1024]{1,0:T(8,128)(2,1)S(1)}, u32[]{:S(2)}, u32[]{:S(2)}) collective-permute-start(bf16[32,1024]{1,0:T(8,128)(2,1)S(1)} %collective-permute-done.3), channel_id=1, source_target_pairs={{0,7},{1,0},{2,1},{3,2},{4,3},{5,4},{6,5},{7,6},{8,15},{9,8},{10,9... | collective-permute-start | bytes 196616 | tf_op jit(solution)/shard_map/ppermute | solution.py:24
  27.5 28.4 %collective-permute-start.6 = (bf16[32,1024]{1,0:T(8,128)(2,1)S(1)}, bf16[32,1024]{1,0:T(8,128)(2,1)S(1)}, u32[]{:S(2)}, u32[]{:S(2)}) collective-permute-start(bf16[32,1024]{1,0:T(8,128)(2,1)S(1)} %collective-permute-done.4), channel_id=1, source_target_pairs={{0,1},{1,2},{2,3},{3,4},{4,5},{5,6},{6,7},{7,0},{8,9},{9,10},{10,1... | collective-permute-start | bytes 196616 | tf_op jit(solution)/shard_map/ppermute | solution.py:21
  40.6 26.9 %collective-permute-start.9 = (bf16[32,1024]{1,0:T(8,128)(2,1)S(1)}, bf16[32,1024]{1,0:T(8,128)(2,1)S(1)}, u32[]{:S(2)}, u32[]{:S(2)}) collective-permute-start(bf16[32,1024]{1,0:T(8,128)(2,1)S(1)} %collective-permute-done.7), channel_id=1, source_target_pairs={{0,1},{1,2},{2,3},{3,4},{4,5},{5,6},{6,7},{7,0},{8,9},{9,10},{10,1... | collective-permute-start | bytes 196616 | tf_op jit(solution)/shard_map/ppermute | solution.py:21
  59.0 158.2 %all-to-all-start = ((bf16[256,4,256]{0,2,1:T(8,128)(2,1)}), bf16[256,4,256]{0,2,1:T(8,128)(2,1)S(1)}, u32[]{:S(2)}, u32[]{:S(2)}) async-start(bf16[256,4,256]{0,2,1:T(8,128)(2,1)} %bitcast.3), calls=%async_computation | async-start | bytes 1048576 | tf_op jit(solution)/shard_map/all_to_all | solution.py:54
  64.2 24.6 %collective-permute-start.10 = (bf16[32,1024]{1,0:T(8,128)(2,1)S(1)}, bf16[32,1024]{1,0:T(8,128)(2,1)S(1)}, u32[]{:S(2)}, u32[]{:S(2)}) collective-permute-start(bf16[32,1024]{1,0:T(8,128)(2,1)S(1)} %collective-permute-done.8), channel_id=1, source_target_pairs={{0,7},{1,0},{2,1},{3,2},{4,3},{5,4},{6,5},{7,6},{8,15},{9,8},{10,9... | collective-permute-start | bytes 196616 | tf_op jit(solution)/shard_map/ppermute | solution.py:24
  67.4 24.9 %collective-permute-start.11 = (bf16[32,1024]{1,0:T(8,128)(2,1)S(1)}, bf16[32,1024]{1,0:T(8,128)(2,1)S(1)}, u32[]{:S(2)}, u32[]{:S(2)}) collective-permute-start(bf16[32,1024]{1,0:T(8,128)(2,1)S(1)} %collective-permute-done.9), channel_id=1, source_target_pairs={{0,1},{1,2},{2,3},{3,4},{4,5},{5,6},{6,7},{7,0},{8,9},{9,10},{10,1... | collective-permute-start | bytes 196616 | tf_op jit(solution)/shard_map/ppermute | solution.py:21
  88.7 121.4 %collective-permute-start.12 = (bf16[32,1024]{1,0:T(8,128)(2,1)S(1)}, bf16[32,1024]{1,0:T(8,128)(2,1)S(1)}, u32[]{:S(2)}, u32[]{:S(2)}) collective-permute-start(bf16[32,1024]{1,0:T(8,128)(2,1)S(1)} %collective-permute-done.10), channel_id=1, source_target_pairs={{0,7},{1,0},{2,1},{3,2},{4,3},{5,4},{6,5},{7,6},{8,15},{9,8},{10,9... | collective-permute-start | bytes 196616 | tf_op jit(solution)/shard_map/ppermute | solution.py:24
  92.3 121.9 %collective-permute-start.13 = (bf16[32,1024]{1,0:T(8,128)(2,1)S(1)}, bf16[32,1024]{1,0:T(8,128)(2,1)S(1)}, u32[]{:S(2)}, u32[]{:S(2)}) collective-permute-start(bf16[32,1024]{1,0:T(8,128)(2,1)S(1)} %collective-permute-done.11), channel_id=1, source_target_pairs={{0,1},{1,2},{2,3},{3,4},{4,5},{5,6},{6,7},{7,0},{8,9},{9,10},{10,1... | collective-permute-start | bytes 196616 | tf_op jit(solution)/shard_map/ppermute | solution.py:21
  217.2 184.8 %all-to-all-start.2 = ((bf16[256,4,256]{0,2,1:T(8,128)(2,1)}), bf16[256,4,256]{0,2,1:T(8,128)(2,1)}, u32[]{:S(2)}, u32[]{:S(2)}) async-start(bf16[256,4,256]{0,2,1:T(8,128)(2,1)} %bitcast.62), calls=%async_computation.3 | async-start | bytes 1048576 | tf_op jit(solution)/shard_map/all_to_all | solution.py:54
  402.0 163.5 %all-to-all-start.1 = ((f32[4,8,32,256]{3,2,1,0:T(8,128)}), f32[4,8,32,256]{3,2,1,0:T(8,128)}, u32[]{:S(2)}, u32[]{:S(2)}) async-start(f32[4,8,32,256]{3,2,1,0:T(8,128)} %bitcast.54), calls=%async_computation.1 | async-start | bytes 2097152 | tf_op jit(solution)/shard_map/all_to_all | solution.py:115
  406.2 195.7 %reduce-scatter.3.cloned.1.call-start = ((), (), s32[]{:S(2)}) async-start(), calls=%async_computation.6 | async-start | bytes 1179648 | tf_op jit(solution)/shard_map/reduce_scatter | solution.py:116
  454.1 4.8 copy-start.27
  470.6 4.8 copy-start.27
  487.2 4.8 copy-start.27
  503.7 4.8 copy-start.27
  520.2 4.8 copy-start.27
  536.7 4.8 copy-start.27
  567.9 66.9 %reduce-scatter.5.cloned.1.call-start = ((), (), s32[]{:S(2)}) async-start(), calls=%async_computation.7 | async-start | bytes 1179648 | tf_op jit(solution)/shard_map/reduce_scatter | solution.py:116
  593.0 44.0 %copy-start.7 = (bf16[32,2048]{1,0:T(8,128)(2,1)S(1)}, bf16[32,2048]{1,0:T(8,128)(2,1)}, u32[]{:S(2)}) copy-start(bf16[32,2048]{1,0:T(8,128)(2,1)} %copy-done.6) | copy-start | bytes 393220
  594.1 44.3 %copy-start.9 = (bf16[32,2048]{1,0:T(8,128)(2,1)S(1)}, bf16[32,2048]{1,0:T(8,128)(2,1)}, u32[]{:S(2)}) copy-start(bf16[32,2048]{1,0:T(8,128)(2,1)} %copy-done.8) | copy-start | bytes 393220
  (99 other events, 306.7 us)
Sparse Core Ops, SparseCore 0:
  568.1 33.8 reduce-scatter.2
  604.2 30.5 reduce-scatter.4
